TPU v7x, 32 devices: a whole 2x2x4 slice. The times are simulated.
32 devices in a mesh: groups: 2 (over y), rows: 4 (over z), cols: 4 (over x, core).
Axes of the slice: x: 2, y: 2, z: 4, core: 2. Of those that a mesh axis runs over, the one named last changes fastest.
Arguments:
- points: bfloat16 [6144, 128], P(('groups', 'rows', 'cols')), parts along dimension 0, as said below
- solution: float32 [6144, 128], P(('groups', 'rows', 'cols')), parts along dimension 0, may hold values from -6 to 6
- targets: float32 [6144, 128], P(('groups', 'rows', 'cols')), parts along dimension 0, may hold values from -40 to 40, as said below
- inducing: int32 [2048], P('groups'), parts along dimension 0, may hold values from 0 to 3071, as said below
- woodbury_inverse: float32 [2048, 1024], P('groups'), parts along dimension 0, may hold values from -1 to 7, as said below
Outputs:
- new_solution: float32 [6144, 128], P(('groups', 'rows', 'cols')), parts along dimension 0
- residual: float32 [6144, 128], P(('groups', 'rows', 'cols')), parts along dimension 0
- relative_norm: float32 [256], P('groups'), parts along dimension 0
There are 2 independent parts, one for each index of `groups`. A program takes and returns all parts, laid end to end along the dimension named above; each array names one. Nothing has to cross between parts.
Inputs may be any that keep to these rules, and one draw needn't show every extreme that they name: `points`: input locations. targets of each right-hand side have their own scale. `inducing`: indices into this problem's points. `woodbury_inverse`: symmetric.
All inputs are finite; a program needn't handle non-finite values.
Results may differ from a plain program's by a relative error of at most 0.0031.
Values may be sent and summed in bfloat16 or wider, within the bound.
No kernel may reach another device: no remote copies, remote signals or barrier semaphores. Data moves between devices by JAX's collectives and lax.ppermute only.
A program may use at most 64 MiB of HBM per device.

v0:
```python
import jax
import jax.numpy as jnp
from jax import lax
from jax.sharding import PartitionSpec as P

F = 128


noise_level = 0.5


def square_norms(values):
    return jnp.sum(jnp.square(values.astype(jnp.float32)), axis=1)


def rbf_tile(left_x, left_sq, right_x, right_sq, gamma):
    inner = lax.dot_general(
        left_x, right_x, (((1,), (1,)), ((), ())), preferred_element_type=jnp.float32
    )
    return jnp.exp(-gamma * (left_sq[:, None] + right_sq[None, :] - 2.0 * inner)).astype(
        jnp.bfloat16
    )


def make_folder(block_x, gamma, pieces):
    block_sq = square_norms(block_x)
    piece_x, piece_v = pieces
    kernel = rbf_tile(block_x, block_sq, piece_x, square_norms(piece_x), gamma)
    return jnp.dot(kernel, piece_v, preferred_element_type=jnp.float32)


def local(points, solution, targets, inducing, woodbury_inverse):
    gamma = 2.5 / F
    local_count = points.shape[0]
    solution_b = solution.astype(jnp.bfloat16)
    block_x = lax.all_gather(points, "cols", axis=0, tiled=True)
    partial_value = make_folder(
        block_x,
        gamma,
        (
            lax.all_gather(points, "rows", axis=0, tiled=True),
            lax.all_gather(solution_b, "rows", axis=0, tiled=True),
        ),
    )
    kernel_product = lax.psum_scatter(partial_value, "cols", scatter_dimension=0, tiled=True)
    residual = targets - kernel_product - noise_level * solution
    offset = (lax.axis_index("rows") * lax.axis_size("cols") + lax.axis_index("cols")) * local_count
    local_ids = offset + jnp.arange(local_count, dtype=jnp.int32)
    selector = (inducing[:, None] == local_ids[None, :]).astype(jnp.bfloat16)
    picked = jnp.dot(selector, points, preferred_element_type=jnp.float32)
    centers = lax.psum(picked, ("rows", "cols")).astype(jnp.bfloat16)
    cross = rbf_tile(points, square_norms(points), centers, square_norms(centers), gamma)
    residual_b = residual.astype(jnp.bfloat16)
    projected_local = lax.dot_general(
        cross, residual_b, (((0,), (0,)), ((), ())), preferred_element_type=jnp.float32
    )
    res_local = jnp.sum(residual * residual, axis=0)
    tar_local = jnp.sum(targets * targets, axis=0)
    share_rows = lax.psum_scatter(projected_local, "rows", scatter_dimension=0, tiled=True)
    share, res_part, tar_part = lax.psum((share_rows, res_local, tar_local), "cols")
    span = share.shape[0]
    begin = lax.axis_index("rows") * span
    inverse_cols = lax.dynamic_slice_in_dim(woodbury_inverse, begin, span, 1)
    weight_part = jnp.dot(inverse_cols, share, precision=lax.Precision.HIGHEST)
    weights, res_sq, tar_sq = lax.psum((weight_part, res_part, tar_part), "rows")
    correction = jnp.dot(cross, weights.astype(jnp.bfloat16), preferred_element_type=jnp.float32)
    new_solution = solution + (residual - correction) / noise_level
    relative_norm = jnp.sqrt(res_sq / (tar_sq + 1e-06))
    return (new_solution, residual, relative_norm)


def solution(mesh):
    return jax.shard_map(
        local,
        mesh=mesh,
        in_specs=(
            P(("groups", "rows", "cols"), None),
            P(("groups", "rows", "cols"), None),
            P(("groups", "rows", "cols"), None),
            P("groups"),
            P("groups", None),
        ),
        out_specs=(
            P(("groups", "rows", "cols"), None),
            P(("groups", "rows", "cols"), None),
            P("groups"),
        ),
        check_vma=False,
    )
```

profile of v0, /device:TPU:0, one launch (start us, length us, event | category | flops | bytes accessed | tf_op | source)
XLA Modules:
  0.0 204.4 jit_solution(171352849018245425)
XLA Ops:
  7.2 0.0 reduce-scatter.3.cloned.1.call-start
  7.2 15.7 %all_gather.10 = bf16[768,128]{1,0:T(8,128)(2,1)S(1)} all-gather(bf16[192,128]{1,0:T(8,128)(2,1)} %param.5), channel_id=1, replica_groups=mesh['groups'=2,'rows'=4,'cols'=4] {'rows'}, dimensions={0}, use_global_device_ids=true | all-gather | bytes 245760 | tf_op jit(solution)/shard_map/all_gather | solution.py:41
  22.9 5.8 %all_gather.9 = bf16[768,128]{1,0:T(8,128)(2,1)S(1)} all-gather(bf16[192,128]{1,0:T(8,128)(2,1)} %param.5), channel_id=1, replica_groups=mesh['groups'=2,'rows'=4,'cols'=4] {'cols'}, dimensions={0}, use_global_device_ids=true | all-gather | bytes 245760 | tf_op jit(solution)/shard_map/all_gather | solution.py:36
  28.7 0.9 convert_element_type.34
  29.6 13.6 %all_gather.11 = bf16[768,128]{1,0:T(8,128)(2,1)S(1)} all-gather(bf16[192,128]{1,0:T(8,128)(2,1)S(1)} %convert_element_type.34), channel_id=1, replica_groups=mesh['groups'=2,'rows'=4,'cols'=4] {'rows'}, dimensions={0}, use_global_device_ids=true | all-gather | bytes 245760 | tf_op jit(solution)/shard_map/all_gather | solution.py:42
  43.2 0.0 copy-start.2
  43.2 0.0 copy-start.4
  43.2 0.2 multiply_reduce_fusion.1
  43.4 0.2 multiply_reduce_fusion.2
  43.6 1.6 fusion
  45.2 0.0 copy-start
  45.2 0.0 copy-start.3
  45.2 0.0 reduce-scatter.3.cloned.1.call-update
  45.2 0.0 reduce-scatter.5.cloned.1.call-start
  45.3 0.0 copy-done.2
  45.3 0.0 copy-done.4
  45.3 0.3 fusion.14
  45.7 0.1 multiply_reduce_fusion.5
  45.8 64.6 %all-reduce.7 = bf16[1024,128]{1,0:T(8,128)(2,1)S(1)} all-reduce(f32[1024,128]{1,0:T(8,128)S(1)} %fusion.14), channel_id=1, replica_groups=mesh['groups'=2,'rows'=4,'cols'=4] {'rows','cols'}, use_global_device_ids=true, to_apply=%region_4.0 | all-reduce | flops 131072 | bytes 786432 | tf_op jit(solution)/shard_map/psum | solution.py:51
  110.5 0.2 multiply_reduce_fusion
  110.7 0.3 fusion.5
  111.0 0.0 reduce-scatter.3.cloned.1.call-done
  111.0 0.0 copy-done
  111.0 0.0 copy-done.3
  111.1 0.9 multiply_reduce_fusion.4
  112.0 0.0 copy-start.1
  112.0 1.1 fusion.20
  113.1 0.0 reduce-scatter.5.cloned.1.call-update
  113.2 0.0 all-reduce.6.cloned.1.call-start
  113.2 19.2 %reduce-scatter.5.cloned.1.call-done = f32[256,128]{1,0:T(8,128)} async-done(((f32[1024,128]{1,0:T(8,128)}), f32[256,128]{1,0:T(8,128)}) %reduce-scatter.5.cloned.1.call-update) | async-done | bytes 131088 | tf_op jit(solution)/shard_map/reduce_scatter | solution.py:59
  132.4 0.0 all-reduce.6.cloned.1.call-update
  132.5 5.7 %all-reduce = (f32[128]{0:T(128)S(1)}, f32[128]{0:T(128)S(1)}) all-reduce(f32[128]{0:T(128)S(1)} %get-tuple-element.8, f32[128]{0:T(128)S(1)} %get-tuple-element.10), channel_id=1, replica_groups=mesh['groups'=2,'rows'=4,'cols'=4] {'cols'}, use_global_device_ids=true, to_apply=%region_10.0 | all-reduce | flops 256 | bytes 2048 | tf_op jit(solution)/shard_map/psum | solution.py:60
  138.1 26.7 %all-reduce.6.cloned.1.call-done = f32[256,128]{1,0:T(8,128)} async-done(((f32[256,128]{1,0:T(8,128)}), f32[256,128]{1,0:T(8,128)}) %all-reduce.6.cloned.1.call-update) | async-done | bytes 131088 | tf_op jit(solution)/shard_map/psum | solution.py:60
  164.8 2.2 %fusion.12 = f32[1024,128]{1,0:T(8,128)S(1)} fusion(f32[256,128]{1,0:T(8,128)} %all-reduce.6.cloned.1.call-done, f32[1024,1024]{1,0:T(8,128)} %param.9, s32[]{:T(128)S(6)} %select_n.3), kind=kOutput, calls=%fused_computation.15 | convolution fusion | flops 402653184 | bytes 1703940 | tf_op jit(solution)/shard_map/dot_general | solution.py:64
  167.0 29.4 %all-reduce.8 = (bf16[1024,128]{1,0:T(8,128)(2,1)S(1)}, f32[128]{0:T(128)S(1)}, f32[128]{0:T(128)S(1)}) all-reduce(f32[1024,128]{1,0:T(8,128)S(1)} %fusion.12, f32[128]{0:T(128)S(1)} %get-tuple-element.3, f32[128]{0:T(128)S(1)} %get-tuple-element.4), channel_id=1, replica_groups=mesh['groups'=2,'rows'=4,'cols'=4] {'rows'}, use_global_device_ids=true, to_apply=%region_8.0 | all-reduce | flops 131328 | bytes 788480 | tf_op jit(solution)/shard_map/psum | solution.py:65
  196.4 0.9 fusion.11
  197.3 0.0 copy-done.1
  197.3 0.5 fusion.22
  (1 shorter events, 0.0 us)
Async XLA Ops:
  7.2 103.9 %reduce-scatter.3.cloned.1.call-start = ((), (), s32[]{:S(2)}) async-start(), calls=%async_computation.2 | async-start | bytes 491520 | tf_op jit(solution)/shard_map/reduce_scatter | solution.py:45
  43.2 2.1 %copy-start.2 = (bf16[192,128]{1,0:T(8,128)(2,1)S(1)}, bf16[192,128]{1,0:T(8,128)(2,1)}, u32[]{:S(2)}) copy-start(bf16[192,128]{1,0:T(8,128)(2,1)} %param.5) | copy-start | bytes 147460
  43.2 2.1 %copy-start.4 = (s32[1024]{0:T(1024)S(1)}, s32[1024]{0:T(1024)}, u32[]{:S(2)}) copy-start(s32[1024]{0:T(1024)} %param.8) | copy-start | bytes 12292
  45.2 65.8 %copy-start = (f32[192,128]{1,0:T(8,128)S(1)}, f32[192,128]{1,0:T(8,128)}, u32[]{:S(2)}) copy-start(f32[192,128]{1,0:T(8,128)} %param.6) | copy-start | bytes 294916
  45.2 65.8 %copy-start.3 = (f32[192,128]{1,0:T(8,128)S(1)}, f32[192,128]{1,0:T(8,128)}, u32[]{:S(2)}) copy-start(f32[192,128]{1,0:T(8,128)} %param.7) | copy-start | bytes 294916
  45.2 87.2 %reduce-scatter.5.cloned.1.call-start = ((), (), s32[]{:S(2)}) async-start(), calls=%async_computation.3 | async-start | bytes 655360 | tf_op jit(solution)/shard_map/reduce_scatter | solution.py:59
  112.0 85.3 %copy-start.1 = (f32[192,128]{1,0:T(8,128)}, f32[192,128]{1,0:T(8,128)S(1)}, u32[]{:S(2)}) copy-start(f32[192,128]{1,0:T(8,128)S(1)} %get-tuple-element.9) | copy-start | bytes 294916
  113.2 51.6 %all-reduce.6.cloned.1.call-start = ((), (), s32[]{:S(2)}) async-start(), calls=%async_computation.4 | async-start | bytes 262144 | tf_op jit(solution)/shard_map/psum | solution.py:60
Sparse Core Ops, SparseCore 0:
  45.4 22.5 reduce-scatter.2
  113.3 19.0 reduce-scatter.4
  134.7 30.0 all-reduce.5
where the time goes:
time: 205 us; the launch traced here: 204 us
  blocking collectives  135 us (66%)
  waiting for transfers between devices  46 us (22%)
  between operations  13.9 us (7%)
  matrix products  6.56 us (3%)
  other arithmetic  3.04 us (1%)
    psum x1, blocking collectives, local(): centers = lax.psum(picked, ('rows', 'cols')).astype(jnp.bfloat16)  64.6 us
    psum x1, blocking collectives, local(): lax.psum((weight_part, res_part, tar_part), 'rows')  29.4 us
    psum x1, waiting for transfers between devices, local(): lax.psum((share_rows, res_local, tar_local), 'cols')  26.7 us
    reduce_scatter x1, waiting for transfers between devices, local(): lax.psum_scatter(projected_local, 'rows', scatter_dimension=0, tiled=True)  19.2 us
    all_gather x1, blocking collectives, local(): lax.all_gather(points, 'rows', axis=0, tiled=True)  15.7 us
    all_gather x1, blocking collectives, local(): lax.all_gather(solution_b, 'rows', axis=0, tiled=True)  13.6 us
    all_gather x1, blocking collectives, local(): block_x = lax.all_gather(points, 'cols', axis=0, tiled=True)  5.8 us
    psum x1, blocking collectives, local(): lax.psum((share_rows, res_local, tar_local), 'cols')  5.67 us
  transfers between devices with their start and end apart: 3, of which 2 were waited for; matrix products, arithmetic and copies ran while one was open for 0% of the time, Pallas kernels for 0%

commit v1 on v0

v1 whole, which is shorter than its diff:
```python
import jax
import jax.numpy as jnp
from jax import lax
from jax.sharding import PartitionSpec as P

F = 128

noise_level = 0.5

COLUMN_CHUNK = 3072


def square_norms(values):
    return jnp.sum(jnp.square(values.astype(jnp.float32)), axis=1)


def rbf_tile(left_x, left_sq, right_x, right_sq, gamma):
    inner = lax.dot_general(
        left_x, right_x, (((1,), (1,)), ((), ())), preferred_element_type=jnp.float32
    )
    return jnp.exp(-gamma * (left_sq[:, None] + right_sq[None, :] - 2.0 * inner)).astype(
        jnp.bfloat16
    )


def kernel_product(own_x, own_sq, all_x, all_sq, all_v, gamma):
    total = all_x.shape[0]
    chunk = min(COLUMN_CHUNK, total)
    if total % chunk != 0:
        chunk = total
    steps = total // chunk

    def piece(start):
        x = lax.dynamic_slice_in_dim(all_x, start, chunk, 0)
        s = lax.dynamic_slice_in_dim(all_sq, start, chunk, 0)
        v = lax.dynamic_slice_in_dim(all_v, start, chunk, 0)
        k = rbf_tile(own_x, own_sq, x, s, gamma)
        return jnp.dot(k, v, preferred_element_type=jnp.float32)

    if steps == 1:
        return piece(0)

    def body(i, acc):
        return acc + piece(i * chunk)

    init = jnp.zeros((own_x.shape[0], all_v.shape[1]), jnp.float32)
    return lax.fori_loop(0, steps, body, init)


def local(points, solution, targets, inducing, woodbury_inverse):
    gamma = 2.5 / F
    solution_b = solution.astype(jnp.bfloat16)
    packed = jnp.concatenate([points, solution_b], axis=1)
    gathered = lax.all_gather(packed, ("rows", "cols"), axis=0, tiled=True)
    all_x = gathered[:, :F]
    all_v = gathered[:, F:]
    all_sq = square_norms(all_x)
    own_sq = square_norms(points)
    kp = kernel_product(points, own_sq, all_x, all_sq, all_v, gamma)
    residual = targets - kp - noise_level * solution
    centers = jnp.take(all_x, inducing, axis=0)
    cross = rbf_tile(points, own_sq, centers, square_norms(centers), gamma)
    residual_b = residual.astype(jnp.bfloat16)
    projected_local = lax.dot_general(
        cross, residual_b, (((0,), (0,)), ((), ())), preferred_element_type=jnp.float32
    )
    res_local = jnp.sum(residual * residual, axis=0)
    tar_local = jnp.sum(targets * targets, axis=0)
    stacked = jnp.concatenate([projected_local, res_local[None], tar_local[None]], axis=0)
    summed = lax.psum(stacked, ("rows", "cols"))
    m = projected_local.shape[0]
    projected = summed[:m]
    res_sq = summed[m]
    tar_sq = summed[m + 1]
    weights = jnp.dot(woodbury_inverse, projected, precision=lax.Precision.HIGHEST)
    correction = jnp.dot(cross, weights.astype(jnp.bfloat16), preferred_element_type=jnp.float32)
    new_solution = solution + (residual - correction) / noise_level
    relative_norm = jnp.sqrt(res_sq / (tar_sq + 1e-06))
    return (new_solution, residual, relative_norm)


def solution(mesh):
    return jax.shard_map(
        local,
        mesh=mesh,
        in_specs=(
            P(("groups", "rows", "cols"), None),
            P(("groups", "rows", "cols"), None),
            P(("groups", "rows", "cols"), None),
            P("groups"),
            P("groups", None),
        ),
        out_specs=(
            P(("groups", "rows", "cols"), None),
            P(("groups", "rows", "cols"), None),
            P("groups"),
        ),
        check_vma=False,
    )
```

time: 205 us -> 168 us (0.82)
  blocking collectives: 135 us -> 0 us
  waiting for transfers between devices: 46 us -> 130 us
  local copies, waits for them, and re-layouts: 0.02 us -> 5.84 us
  other arithmetic: 3.04 us -> 7.78 us
  matrix products: 6.56 us -> 9.52 us
    psum x3 -> x0, blocking collectives: 99.7 us -> none  [the longest x1 64.6 us: local(): centers = lax.psum(picked, ('rows', 'cols')).astype(jnp.bfloat16)]
    psum x1, waiting for transfers between devices: 26.7 us -> 89.5 us  [local(): summed = lax.psum(stacked, ('rows', 'cols'))]
    all_gather x0 -> x1, waiting for transfers between devices: none -> 40.2 us  [local(): gathered = lax.all_gather(packed, ('rows', 'cols'), axis=0, tiled=True)]
    all_gather x3 -> x0, blocking collectives: 35.1 us -> none  [the longest x1 15.7 us: local(): lax.all_gather(points, 'rows', axis=0, tiled=True)]
    reduce_scatter x2 -> x0, waiting for transfers between devices: 19.2 us -> none  [the longest x1 19.2 us: local(): lax.psum_scatter(projected_local, 'rows', scatter_dimension=0, tiled=True)]
    dot_general x3 -> x2, matrix products: 4.2 us -> 7.81 us  [the longest x1 6.82 us: local(): jnp.dot(woodbury_inverse, projected, precision=lax.Precision.HIGHEST)]
    gather x0 -> x1, local copies, waits for them, and re-layouts: none -> 3.2 us  [local(): centers = jnp.take(all_x, inducing, axis=0)]
  transfers between devices with their start and end apart: 3 -> 2, of which waited for: 2 -> 2; matrix products, arithmetic and copies ran while one was open for 0% -> 2% of each run, Pallas kernels for 0% -> 0%
where the time goes in v1:
time: 168 us; the launch traced here: 167 us
  waiting for transfers between devices  130 us (77%)
  between operations  14.1 us (8%)
  matrix products  9.52 us (6%)
  other arithmetic  7.78 us (5%)
  local copies, waits for them, and re-layouts  5.84 us (3%)
    psum x1, waiting for transfers between devices, local(): summed = lax.psum(stacked, ('rows', 'cols'))  89.5 us
    all_gather x1, waiting for transfers between devices, local(): gathered = lax.all_gather(packed, ('rows', 'cols'), axis=0, tiled=True)  40.2 us
    dot_general x1, matrix products, local(): jnp.dot(woodbury_inverse, projected, precision=lax.Precision.HIGHEST)  6.82 us
  transfers between devices with their start and end apart: 2, of which 2 were waited for; matrix products, arithmetic and copies ran while one was open for 2% of the time, Pallas kernels for 0%

profile of v1, /device:TPU:0, one launch (start us, length us, event | category | flops | bytes accessed | tf_op | source)
XLA Modules:
  0.0 167.1 jit_solution(9886940378741417680)
XLA Ops:
  7.2 0.0 all-gather.2.cloned.1.call-start
  7.2 0.9 convert_element_type.26
  8.1 0.0 copy-start.3
  8.1 1.5 pad_maximum_fusion
  9.6 0.0 all-gather.2.cloned.1.call-update
  9.7 0.0 all-reduce.2.cloned.1.call-start
  9.7 0.9 multiply_reduce_fusion.4
  10.6 0.9 multiply_reduce_fusion.2
  11.6 0.7 compare_and_fusion
  12.3 0.7 fusion.23
  12.9 40.2 %all-gather.2.cloned.1.call-done = bf16[3072,256]{1,0:T(8,128)(2,1)} async-done(((bf16[192,256]{1,0:T(8,128)(2,1)}), bf16[3072,256]{1,0:T(8,128)(2,1)}) %all-gather.2.cloned.1.call-update) | async-done | bytes 1572880 | tf_op jit(solution)/shard_map/all_gather | solution.py:54
  53.2 0.0 slice-start
  53.2 1.1 slice-done
  54.3 0.0 copy-start
  54.3 0.0 copy-start.1
  54.3 0.0 copy-start.4
  54.3 3.2 %gather_fusion = bf16[1024,128]{1,0:T(8,128)(2,1)S(1)} fusion(bf16[3072,128]{1,0:T(8,128)(2,1)S(1)} %slice-done, s32[1024]{0:T(1024)S(1)} %fusion.23), kind=kCustom, calls=%fused_computation | custom fusion | bytes 528384 | tf_op jit(solution)/shard_map/jit(_take)/gather | solution.py:61
  57.5 0.4 multiply_reduce_fusion.1
  57.9 0.0 copy-done.3
  57.9 0.5 fusion.10
  58.4 0.0 copy-done
  58.4 0.5 multiply_reduce_fusion
  58.9 0.0 copy-done.1
  58.9 0.0 copy-done.4
  58.9 1.0 multiply_reduce_fusion.3
  59.9 0.0 copy-start.2
  59.9 0.3 fusion.21
  60.2 1.5 concatenate.7
  61.7 0.0 all-reduce.2.cloned.1.call-update
  61.7 89.5 %all-reduce.2.cloned.1.call-done = f32[1026,128]{1,0:T(8,128)} async-done(((f32[1026,128]{1,0:T(8,128)}), f32[1026,128]{1,0:T(8,128)}) %all-reduce.2.cloned.1.call-update) | async-done | bytes 525328 | tf_op jit(solution)/shard_map/psum | solution.py:70
  151.3 6.8 %convolution_convert_fusion = bf16[128,1024]{1,0:T(8,128)(2,1)S(1)} fusion(f32[1024,1024]{1,0:T(8,128)} %param.9, f32[1026,128]{1,0:T(8,128)} %all-reduce.2.cloned.1.call-done), kind=kOutput, calls=%fused_computation.15 | convolution fusion | flops 1610743808 | bytes 4980736 | tf_op jit(solution)/shard_map/dot_general | solution.py:75
  158.1 0.0 copy-done.2
  158.1 0.9 fusion.18
  159.0 1.3 sqrt_bitcast_fusion
Async XLA Ops:
  7.2 46.0 %all-gather.2.cloned.1.call-start = ((), (), s32[]{:S(2)}) async-start(), calls=%async_computation | async-start | bytes 1671168 | tf_op jit(solution)/shard_map/all_gather | solution.py:54
  8.1 49.8 %copy-start.3 = (bf16[192,128]{1,0:T(8,128)(2,1)S(1)}, bf16[192,128]{1,0:T(8,128)(2,1)}, u32[]{:S(2)}) copy-start(bf16[192,128]{1,0:T(8,128)(2,1)} %param.5) | copy-start | bytes 147460
  9.7 141.6 %all-reduce.2.cloned.1.call-start = ((), (), s32[]{:S(2)}) async-start(), calls=%async_computation.1 | async-start | bytes 1056768 | tf_op jit(solution)/shard_map/psum | solution.py:70
  53.2 1.1 slice-start
  54.3 4.1 %copy-start = (bf16[3072,256]{1,0:T(8,128)(2,1)S(1)}, bf16[3072,256]{1,0:T(8,128)(2,1)}, u32[]{:S(2)}) copy-start(bf16[3072,256]{1,0:T(8,128)(2,1)} %all-gather.2.cloned.1.call-done) | copy-start | bytes 4718596
  54.3 4.5 %copy-start.1 = (f32[192,128]{1,0:T(8,128)S(1)}, f32[192,128]{1,0:T(8,128)}, u32[]{:S(2)}) copy-start(f32[192,128]{1,0:T(8,128)} %param.6) | copy-start | bytes 294916
  54.3 4.6 %copy-start.4 = (f32[192,128]{1,0:T(8,128)S(1)}, f32[192,128]{1,0:T(8,128)}, u32[]{:S(2)}) copy-start(f32[192,128]{1,0:T(8,128)} %param.7) | copy-start | bytes 294916
  59.9 98.2 %copy-start.2 = (f32[192,128]{1,0:T(8,128)}, f32[192,128]{1,0:T(8,128)S(1)}, u32[]{:S(2)}) copy-start(f32[192,128]{1,0:T(8,128)S(1)} %get-tuple-element.4) | copy-start | bytes 294916
Sparse Core Ops, SparseCore 0:
  10.8 42.3 all-gather.1
  61.9 89.3 all-reduce.1

commit v2 on v1

--- a/solution.py
+++ b/solution.py
@@ -47,8 +47,39 @@
     return lax.fori_loop(0, steps, body, init)
 
 
+def split_bf16(values):
+    hi = values.astype(jnp.bfloat16)
+    lo = (values - hi.astype(jnp.float32)).astype(jnp.bfloat16)
+    return hi, lo
+
+
+def projected_all(all_x, all_sq, centers, centers_sq, residual_b_all, gamma):
+    total = all_x.shape[0]
+    chunk = min(COLUMN_CHUNK, total)
+    if total % chunk != 0:
+        chunk = total
+    steps = total // chunk
+
+    def piece(start):
+        x = lax.dynamic_slice_in_dim(all_x, start, chunk, 0)
+        s = lax.dynamic_slice_in_dim(all_sq, start, chunk, 0)
+        r = lax.dynamic_slice_in_dim(residual_b_all, start, chunk, 0)
+        c = rbf_tile(x, s, centers, centers_sq, gamma)
+        return lax.dot_general(c, r, (((0,), (0,)), ((), ())), preferred_element_type=jnp.float32)
+
+    if steps == 1:
+        return piece(0)
+
+    def body(i, acc):
+        return acc + piece(i * chunk)
+
+    init = jnp.zeros((centers.shape[0], residual_b_all.shape[1]), jnp.float32)
+    return lax.fori_loop(0, steps, body, init)
+
+
 def local(points, solution, targets, inducing, woodbury_inverse):
     gamma = 2.5 / F
+    n_local = points.shape[0]
     solution_b = solution.astype(jnp.bfloat16)
     packed = jnp.concatenate([points, solution_b], axis=1)
     gathered = lax.all_gather(packed, ("rows", "cols"), axis=0, tiled=True)
@@ -59,19 +90,24 @@
     kp = kernel_product(points, own_sq, all_x, all_sq, all_v, gamma)
     residual = targets - kp - noise_level * solution
     centers = jnp.take(all_x, inducing, axis=0)
-    cross = rbf_tile(points, own_sq, centers, square_norms(centers), gamma)
+    centers_sq = square_norms(centers)
+    cross = rbf_tile(points, own_sq, centers, centers_sq, gamma)
     residual_b = residual.astype(jnp.bfloat16)
-    projected_local = lax.dot_general(
-        cross, residual_b, (((0,), (0,)), ((), ())), preferred_element_type=jnp.float32
-    )
     res_local = jnp.sum(residual * residual, axis=0)
     tar_local = jnp.sum(targets * targets, axis=0)
-    stacked = jnp.concatenate([projected_local, res_local[None], tar_local[None]], axis=0)
-    summed = lax.psum(stacked, ("rows", "cols"))
-    m = projected_local.shape[0]
-    projected = summed[:m]
-    res_sq = summed[m]
-    tar_sq = summed[m + 1]
+    hi, lo = split_bf16(jnp.stack([res_local, tar_local]))
+    pad = jnp.zeros((12, residual_b.shape[1]), jnp.bfloat16)
+    sent = jnp.concatenate([residual_b, hi, lo, pad], axis=0)
+    rows_sent = sent.shape[0]
+    got = lax.all_gather(sent, ("rows", "cols"), axis=0, tiled=False)
+    residual_b_all = got[:, :n_local].reshape(-1, residual_b.shape[1])
+    norm_parts = got[:, n_local:n_local + 2].astype(jnp.float32) + got[:, n_local + 2:n_local + 4].astype(
+        jnp.float32
+    )
+    norms = jnp.sum(norm_parts, axis=0)
+    res_sq = norms[0]
+    tar_sq = norms[1]
+    projected = projected_all(all_x, all_sq, centers, centers_sq, residual_b_all, gamma)
     weights = jnp.dot(woodbury_inverse, projected, precision=lax.Precision.HIGHEST)
     correction = jnp.dot(cross, weights.astype(jnp.bfloat16), preferred_element_type=jnp.float32)
     new_solution = solution + (residual - correction) / noise_level

time: 168 us -> 105 us (0.62)
  waiting for transfers between devices: 130 us -> 40.3 us
  blocking collectives: 0 us -> 21.6 us
  matrix products: 9.52 us -> 16.6 us
  local copies, waits for them, and re-layouts: 5.84 us -> 3.37 us
    psum x1 -> x0, waiting for transfers between devices: 89.5 us -> none  [local(): summed = lax.psum(stacked, ('rows', 'cols'))]
    all_gather x0 -> x1, blocking collectives: none -> 21.6 us  [local(): got = lax.all_gather(sent, ('rows', 'cols'), axis=0, tiled=False)]
    dot_general x2 -> x1, matrix products: 0.8 us -> 6.24 us  [piece(): lax.dot_general(c, r, (((0,), (0,)), ((), ())), preferred_element_type=jn...]
  transfers between devices with their start and end apart: 2 -> 1, of which waited for: 2 -> 1; matrix products, arithmetic and copies ran while one was open for 2% -> 3% of each run, Pallas kernels for 0% -> 0%
where the time goes in v2:
time: 105 us; the launch traced here: 104 us
  waiting for transfers between devices  40.3 us (38%)
  blocking collectives  21.6 us (21%)
  matrix products  16.6 us (16%)
  between operations  14.2 us (14%)
  other arithmetic  8.23 us (8%)
  local copies, waits for them, and re-layouts  3.37 us (3%)
    all_gather x1, waiting for transfers between devices, local(): gathered = lax.all_gather(packed, ('rows', 'cols'), axis=0, tiled=True)  40.3 us
    all_gather x1, blocking collectives, local(): got = lax.all_gather(sent, ('rows', 'cols'), axis=0, tiled=False)  21.6 us
    dot_general x1, matrix products, local(): jnp.dot(woodbury_inverse, projected, precision=lax.Precision.HIGHEST)  6.7 us
    dot_general x1, matrix products, piece(): lax.dot_general(c, r, (((0,), (0,)), ((), ())), preferred_element_type=jn...  6.24 us
    gather x1, local copies, waits for them, and re-layouts, local(): centers = jnp.take(all_x, inducing, axis=0)  3.2 us
    reduce_sum x3, other arithmetic, square_norms(): return jnp.sum(jnp.square(values.astype(jnp.float32)), axis=1)  2.88 us
    dot_general x1, matrix products, piece(): return jnp.dot(k, v, preferred_element_type=jnp.float32)  2.45 us
  transfers between devices with their start and end apart: 1, of which 1 were waited for; matrix products, arithmetic and copies ran while one was open for 3% of the time, Pallas kernels for 0%

profile of v2, /device:TPU:0, one launch (start us, length us, event | category | flops | bytes accessed | tf_op | source)
XLA Modules:
  0.0 104.3 jit_solution(14330210817890078864)
XLA Ops:
  7.2 0.0 all-gather.3.cloned.1.call-start
  7.2 0.9 convert_element_type.44
  8.1 1.5 %pad_maximum_fusion = bf16[192,256]{1,0:T(8,128)(2,1)} fusion(bf16[192,128]{1,0:T(8,128)(2,1)S(1)} %convert_element_type.44, bf16[192,128]{1,0:T(8,128)(2,1)} %param.5), kind=kLoop, calls=%fused_computation.36 | loop fusion | flops 196608 | bytes 196608 | tf_op jit(solution)/shard_map/concatenate | solution.py:84
  9.6 0.0 all-gather.3.cloned.1.call-update
  9.6 0.1 pad.3.clone
  9.7 0.9 multiply_reduce_fusion.4
  10.6 0.9 multiply_reduce_fusion.2
  11.5 0.7 compare_and_fusion
  12.2 0.7 fusion.28
  12.9 40.3 %all-gather.3.cloned.1.call-done = bf16[3072,256]{1,0:T(8,128)(2,1)} async-done(((bf16[192,256]{1,0:T(8,128)(2,1)}), bf16[3072,256]{1,0:T(8,128)(2,1)}) %all-gather.3.cloned.1.call-update) | async-done | bytes 1572880 | tf_op jit(solution)/shard_map/all_gather | solution.py:85
  53.2 1.6 %multiply_reduce_fusion = f32[3072]{0:T(1024)S(1)} fusion(bf16[3072,256]{1,0:T(8,128)(2,1)} %all-gather.3.cloned.1.call-done), kind=kLoop, calls=%fused_computation.9 | loop fusion | flops 1176576 | bytes 798720 | tf_op jit(solution)/shard_map/reduce_sum | solution.py:14
  54.8 2.4 %fusion.40 = (bf16[192,128]{1,0:T(8,128)(2,1)S(1)}, f32[128]{0:T(128)S(1)}, f32[192,128]{1,0:T(8,128)S(1)}) fusion(f32[192,128]{1,0:T(8,128)} %param.6, f32[192,128]{1,0:T(8,128)} %param.7, bf16[3072,256]{1,0:T(8,128)(2,1)} %all-gather.3.cloned.1.call-done, bf16[192,128]{1,0:T(8,128)(2,1)} %param.5, f32[3072]{0:T(1024)S(1)} %multiply_reduce_fusion, ...), kind=kOutput, calls=%fused_computation.58 | convolution fusion | flops 305086336 | bytes 1979648 | tf_op jit(solution)/shard_map/dot_general | solution.py:38
  57.2 0.0 copy-start.3
  57.3 0.0 slice-start
  57.3 0.1 maximum_maximum_fusion
  57.4 21.6 %all-gather = bf16[3328,128]{1,0:T(8,128)(2,1)S(1)} all-gather(bf16[208,128]{1,0:T(8,128)(2,1)S(1)} %maximum_maximum_fusion), channel_id=2, replica_groups=mesh['groups'=2,'rows'=4,'cols'=4] {'rows','cols'}, dimensions={0}, use_global_device_ids=true | all-gather | bytes 905216 | tf_op jit(solution)/shard_map/all_gather | solution.py:102
  79.1 0.1 slice.32
  79.1 0.0 copy-start
  79.1 0.5 sqrt_bitcast_fusion
  79.7 0.0 slice-done
  79.7 3.2 %gather_fusion = bf16[1024,128]{1,0:T(8,128)(2,1)S(1)} fusion(bf16[3072,128]{1,0:T(8,128)(2,1)S(1)} %slice-done, s32[1024]{0:T(1024)S(1)} %fusion.28), kind=kCustom, calls=%fused_computation | custom fusion | bytes 528384 | tf_op jit(solution)/shard_map/jit(_take)/gather | solution.py:92
  82.9 0.4 multiply_reduce_fusion.1
  83.2 0.0 copy-done
  83.3 6.2 %fusion.5 = f32[1024,128]{1,0:T(8,128)S(1)} fusion(bf16[3072,128]{1,0:T(8,128)(2,1)S(1)} %bitcast.50, f32[1024]{0:T(1024)S(1)} %multiply_reduce_fusion.1, f32[3072]{0:T(1024)S(1)} %multiply_reduce_fusion, bf16[1024,128]{1,0:T(8,128)(2,1)S(1)} %gather_fusion, pred[1024]{0:T(1024)(128)(4,1)S(1)} %compare_and_fusion, bf16[3072,256]{1,0:T(8,128)(2,1)S(1)} %copy-done), kind=kOutput, calls=%fused_computation.8 | convolution fusion | flops 1626472448 | bytes 2376704 | tf_op jit(solution)/shard_map/dot_general | solution.py:68
  89.5 0.0 copy-start.1
  89.5 0.0 copy-start.2
  89.5 6.7 %convolution_convert_fusion = bf16[128,1024]{1,0:T(8,128)(2,1)S(1)} fusion(f32[1024,128]{1,0:T(8,128)S(1)} %fusion.5, f32[1024,1024]{1,0:T(8,128)} %param.9), kind=kOutput, calls=%fused_computation.18 | convolution fusion | flops 1610743808 | bytes 4980736 | tf_op jit(solution)/shard_map/dot_general | solution.py:111
  96.2 0.0 copy-done.3
  96.2 0.0 copy-done.1
  96.3 0.0 copy-done.2
  96.3 1.2 %fusion.19 = f32[192,128]{1,0:T(8,128)} fusion(f32[192,128]{1,0:T(8,128)S(1)} %copy-done.2, f32[192,128]{1,0:T(8,128)S(1)} %get-tuple-element.5, bf16[128,1024]{1,0:T(8,128)(2,1)S(1)} %convolution_convert_fusion, bf16[192,128]{1,0:T(8,128)(2,1)S(1)} %copy-done.1, f32[1024]{0:T(1024)S(1)} %multiply_reduce_fusion.1, f32[192]{0:T(256)S(1)} %multiply_reduce_fusion.4, ...), kind=kOutput, calls=%fused_computation.25 | convolution fusion | flops 101851136 | bytes 874240 | tf_op jit(solution)/shard_map/dot_general | solution.py:112
  (4 shorter events, 0.1 us)
Async XLA Ops:
  7.2 46.0 %all-gather.3.cloned.1.call-start = ((), (), s32[]{:S(2)}) async-start(), calls=%async_computation | async-start | bytes 1671168 | tf_op jit(solution)/shard_map/all_gather | solution.py:85
  57.2 39.0 %copy-start.3 = (f32[192,128]{1,0:T(8,128)}, f32[192,128]{1,0:T(8,128)S(1)}, u32[]{:S(2)}) copy-start(f32[192,128]{1,0:T(8,128)S(1)} %get-tuple-element.5) | copy-start | bytes 294916
  57.3 22.4 %slice-start = ((bf16[3072,256]{1,0:T(8,128)(2,1)}), bf16[3072,128]{1,0:T(8,128)(2,1)S(1)}, s32[]{:S(2)}) async-start(bf16[3072,256]{1,0:T(8,128)(2,1)} %all-gather.3.cloned.1.call-done), calls=%async_computation.1 | async-start | bytes 1572864 | tf_op jit(solution)/shard_map/slice | solution.py:86
  79.1 4.1 %copy-start = (bf16[3072,256]{1,0:T(8,128)(2,1)S(1)}, bf16[3072,256]{1,0:T(8,128)(2,1)}, u32[]{:S(2)}) copy-start(bf16[3072,256]{1,0:T(8,128)(2,1)} %all-gather.3.cloned.1.call-done) | copy-start | bytes 4718596
  89.5 6.7 %copy-start.1 = (bf16[192,128]{1,0:T(8,128)(2,1)S(1)}, bf16[192,128]{1,0:T(8,128)(2,1)}, u32[]{:S(2)}) copy-start(bf16[192,128]{1,0:T(8,128)(2,1)} %param.5) | copy-start | bytes 147460
  89.5 6.7 %copy-start.2 = (f32[192,128]{1,0:T(8,128)S(1)}, f32[192,128]{1,0:T(8,128)}, u32[]{:S(2)}) copy-start(f32[192,128]{1,0:T(8,128)} %param.6) | copy-start | bytes 294916
Sparse Core Ops, SparseCore 0:
  10.8 42.3 all-gather.2
